TPU v7x, 256 devices: a whole 4x4x8 slice. The times are simulated.
256 devices in a mesh: person: 2 (over x_lo), tm: 32 (over y, z), mp: 4 (over x_hi, core).
Axes of the slice: x: 4 (x_hi: 2, x_lo: 2; x = x_hi * 2 + x_lo), y: 4, z: 8, core: 2. Of those that a mesh axis runs over, the one named last changes fastest.
Arguments:
- motion: bfloat16 [2, 2, 8192, 2048], P('person', None, 'tm', 'mp'), may hold values from -6 to 6
- valid: int32 [2, 2, 8192], P('person', None, 'tm'), may hold values from 0 to 1, as said below
- windows: int32 [32], replicated, may hold values from 64 to 512, as said below
- gains: float32 [2, 2048], replicated, may hold values from 0.5 to 1.5
- w_self_in: bfloat16 [2048, 3072], P('tm', 'mp')
- w_self_out: bfloat16 [2048, 2048], P('mp', 'tm'), may hold values from -0.125 to 0.125
- w_cross_in: bfloat16 [2048, 3072], P('tm', 'mp')
- w_cross_out: bfloat16 [2048, 2048], P('mp', 'tm'), may hold values from -0.125 to 0.125
Outputs:
- mixed: bfloat16 [2, 2, 8192, 2048], P('person', None, 'tm', 'mp')
Inputs may be any that keep to these rules, and one draw needn't show every extreme that they name: `valid`: for each person and clip the frames with 1 form a prefix that covers at least half of the 8192 frames and never all of them. `windows`: some head's window is exactly 512.
All inputs are finite; a program needn't handle non-finite values.
Results may differ from a plain program's by a relative error of at most 0.035.
The roundings to bfloat16 on the way count: a program that leaves them out, or rounds other values in their place, can miss the bound.
Values may be sent and summed in bfloat16 or wider, within the bound.
No kernel may reach another device: no remote copies, remote signals or barrier semaphores. Data moves between devices by JAX's collectives and lax.ppermute only.
A program may use at most 64 MiB of HBM per device.

v0:
```python
import jax
import jax.numpy as jnp
from jax import lax
from jax.sharding import PartitionSpec as P

D = 2048
HEADS = 32
KV_HEADS = 8
HEAD_DIM = 64
WIN = 512
EPS = 1e-05


def passed_along(value, axis, steps):
    count = lax.axis_size(axis)
    leading, last = (max(0, -steps), min(count, count - steps))
    return lax.ppermute(value, axis, [(source, source + steps) for source in range(leading, last)])


def swapped(value, axis, apart):
    mask = 2**apart
    pairs = [(source, source ^ mask) for source in range(lax.axis_size(axis))]
    return lax.ppermute(value, axis, pairs)


def rms_normed(rows, gain):
    values = rows.astype(jnp.float32)
    scale = lax.rsqrt(jnp.mean(values * values, axis=-1, keepdims=True) + EPS)
    return (values * scale * gain).astype(jnp.bfloat16)


def project_in(normed_rows, weight_rows):
    total = jnp.dot(
        normed_rows,
        lax.all_gather(weight_rows, "tm", axis=0, tiled=True),
        preferred_element_type=jnp.float32,
    )
    return total.astype(jnp.bfloat16)


def earlier_frames(pair, frames):
    pieces = [pair]
    for step in range(1, WIN // frames + 1):
        pieces.insert(0, passed_along((pair[0], pair[1]), "tm", step))
    key_vals = jnp.concatenate([piece[0] for piece in pieces], 1)
    masks = jnp.concatenate([piece[1] for piece in pieces], 1)
    return (key_vals, masks)


def window_attend(queries, key_vals, masks, wins):
    count_q = queries.shape[1]
    count_k = key_vals.shape[1]
    dist = jnp.arange(count_q)[:, None] + (count_k - count_q) - jnp.arange(count_k)[None, :]

    def one_clip(items):
        query, pairs, kvalid = items
        keys = pairs[:, :, 0]
        values = pairs[:, :, 1]
        allowed = (
            (dist >= 0)
            & (dist < wins[:, :, None, None])
            & ((kvalid[None, None, None, :] == 1) | (dist == 0))
        )
        scores = jnp.einsum(
            "qkgd,ckd->kgqc", query, keys, preferred_element_type=jnp.float32
        ) * HEAD_DIM ** (-0.5)
        top = jnp.max(jnp.where(allowed, scores, -1e30), axis=-1, keepdims=True)
        exps = jnp.where(allowed, jnp.exp(scores - top), 0.0)
        total = jnp.sum(exps, axis=-1)
        weights = exps.astype(jnp.bfloat16)
        summed = jnp.einsum("kgqc,ckd->qkgd", weights, values, preferred_element_type=jnp.float32)
        return (summed / jnp.transpose(total, (2, 0, 1))[..., None]).astype(jnp.bfloat16)

    outputs = lax.map(one_clip, (queries, key_vals, masks))
    return outputs.reshape(outputs.shape[0] * outputs.shape[1], -1)


def project_out(heads, weight, residual):
    terms = jnp.dot(
        heads, lax.all_gather(weight, "tm", axis=1, tiled=True), preferred_element_type=jnp.float32
    )
    summed = lax.psum_scatter(terms, "mp", scatter_dimension=1, tiled=True)
    return (residual.astype(jnp.float32) + summed).astype(jnp.bfloat16)


def body(motion, valid, windows, gains, w_self_in, w_self_out, w_cross_in, w_cross_out):
    clips = motion.shape[1]
    frames = motion.shape[2]
    count = clips * frames
    group = HEADS // KV_HEADS
    local_heads = w_self_out.shape[0] // HEAD_DIM
    local_groups = local_heads // group
    wins = lax.dynamic_slice_in_dim(
        windows, lax.axis_index("mp") * local_heads, local_heads, 0
    ).reshape(local_groups, group)
    own_valid = valid[0]
    residual = motion.reshape(count, motion.shape[3])
    full = lax.all_gather(motion, "mp", axis=3, tiled=True).reshape(count, D)
    normed = rms_normed(full, gains[0])
    self_proj = project_in(normed, w_self_in).reshape(
        clips, frames, local_groups, group + 2, HEAD_DIM
    )
    self_pair = self_proj[:, :, :, group:]
    key_vals, masks = earlier_frames((self_pair, own_valid), frames)
    self_heads = window_attend(self_proj[:, :, :, :group], key_vals, masks, wins)
    hidden = project_out(self_heads, w_self_out, residual)
    hidden_full = lax.all_gather(hidden, "mp", axis=1, tiled=True)
    normed2 = rms_normed(hidden_full, gains[1])
    cross_proj = project_in(normed2, w_cross_in).reshape(
        clips, frames, local_groups, group + 2, HEAD_DIM
    )
    cross_pair = cross_proj[:, :, :, group:]
    partner = swapped((cross_pair, own_valid), "person", 0)
    partner_vals, partner_masks = earlier_frames(partner, frames)
    cross_heads = window_attend(cross_proj[:, :, :, :group], partner_vals, partner_masks, wins)
    mixed = project_out(cross_heads, w_cross_out, hidden)
    return mixed.reshape(motion.shape)


def solution(mesh):
    in_specs = (
        P("person", None, "tm", "mp"),
        P("person", None, "tm"),
        P(),
        P(),
        P("tm", "mp"),
        P("mp", "tm"),
        P("tm", "mp"),
        P("mp", "tm"),
    )
    out_specs = P("person", None, "tm", "mp")
    return jax.shard_map(body, mesh=mesh, in_specs=in_specs, out_specs=out_specs, check_vma=False)
```

profile of v0, /device:TPU:1, one launch (start us, length us, event | category | flops | bytes accessed | tf_op | source)
XLA Modules:
  0.0 520.7 jit_solution(5809093448599657538)
XLA Ops:
  6.5 0.7 all-gather.7.cloned.1.call-update
  7.3 0.7 all-gather.9.cloned.1.call-update
  8.1 0.7 all-gather.11.cloned.1.call-update
  8.8 0.8 fusion.121
  9.6 32.9 %all-gather.7.cloned.1.call-done = bf16[1,2,256,2048]{3,2,1,0:T(8,128)(2,1)} async-done(((bf16[1,2,256,512]{3,2,1,0:T(8,128)(2,1)}), bf16[1,2,256,2048]{3,2,1,0:T(8,128)(2,1)}) %all-gather.7.cloned.1.call-update) | async-done | bytes 2097168 | tf_op jit(solution)/shard_map/all_gather | solution.py:98
  42.5 2.2 multiply_reduce_fusion
  44.8 0.5 fusion.102
  45.3 74.5 %all-gather.9.cloned.1.call-done = bf16[2048,768]{1,0:T(8,128)(2,1)} async-done(((bf16[64,768]{1,0:T(8,128)(2,1)}), bf16[2048,768]{1,0:T(8,128)(2,1)}) %all-gather.9.cloned.1.call-update) | async-done | bytes 3145744 | tf_op jit(solution)/shard_map/all_gather | solution.py:35
  119.8 3.7 convolution_convert_fusion
  124.1 3.5 collective-permute-start
  127.6 3.1 collective-permute-start.1
  130.8 3.1 collective-permute-start.2
  133.9 2.4 collective-permute-start.3
  136.4 5.5 %collective-permute-done.2 = s32[2,256]{1,0:T(2,128)S(1)} collective-permute-done((s32[2,256]{1,0:T(2,128)S(1)}, s32[2,256]{1,0:T(2,128)S(1)}, u32[]{:S(2)}, u32[]{:S(2)}) %collective-permute-start.2) | collective-permute-done | bytes 2080 | tf_op jit(solution)/shard_map/ppermute | solution.py:17
  142.4 0.8 pad_maximum_fusion
  143.4 19.0 %while.24 = (s32[]{:T(128)}, bf16[2,256,2,4,64]{1,4,3,2,0:T(8,128)(2,1)S(1)}, bf16[2,768,2,2,64]{1,4,2,3,0:T(8,128)(2,1)S(1)}, s32[8]{0:T(128)S(1)}, s32[2,768]{...) while((s32[]{:T(128)}, ...), condition=%wide.region_4.5_spmd.clone.clone, body=%wide.region_1.4_spmd.clone.clone.sunk | while | flops 625673728 | bytes 12019361 | solution.py:74
  143.9 6.4 %fusion.149 = (f32[2,4,256]{2,1,0:T(4,128)S(1)}, bf16[2,4,256,768]{2,3,1,0:T(8,128)(2,1)}) fusion(s32[2,4]{1,0:T(2,128)S(1)} %lt.125, s32[256,768]{0,1:T(8,128)S(1)} %iota_subtract_fusion.4, pred[256,768]{0,1:T(8,128)(4,1)S(1)} %get-tuple-element.308, pred[256,768]{0,1:T(8,128)(4,1)S(1)} %get-tuple-element.309, ...), kind=kOutput, calls=%fused_computation.100.clone.1 | convolution fusion | flops 423101184 | bytes 6433792 | tf_op jit(solution)/shard_map/while/body/eval_jaxpr/sub | solution.py:68
  150.3 2.5 fusion.150
  153.4 6.4 %fusion.149 = (f32[2,4,256]{2,1,0:T(4,128)S(1)}, bf16[2,4,256,768]{2,3,1,0:T(8,128)(2,1)}) fusion(s32[2,4]{1,0:T(2,128)S(1)} %lt.125, s32[256,768]{0,1:T(8,128)S(1)} %iota_subtract_fusion.4, pred[256,768]{0,1:T(8,128)(4,1)S(1)} %get-tuple-element.308, pred[256,768]{0,1:T(8,128)(4,1)S(1)} %get-tuple-element.309, ...), kind=kOutput, calls=%fused_computation.100.clone.1 | convolution fusion | flops 423101184 | bytes 6433792 | tf_op jit(solution)/shard_map/while/body/eval_jaxpr/sub | solution.py:68
  159.8 2.5 fusion.150
  162.3 0.5 copy.20
  163.0 33.2 %all-gather.11.cloned.1.call-done = bf16[512,2048]{0,1:T(8,128)(2,1)} async-done(((bf16[512,64]{0,1:T(8,128)(2,1)}), bf16[512,2048]{0,1:T(8,128)(2,1)}) %all-gather.11.cloned.1.call-update) | async-done | bytes 2097168 | tf_op jit(solution)/shard_map/all_gather | solution.py:80
  196.2 4.9 fusion.122
  201.2 58.2 %reduce-scatter.3.cloned.1.call-done = f32[512,512]{1,0:T(8,128)} async-done(((f32[512,2048]{1,0:T(8,128)}), f32[512,512]{1,0:T(8,128)}) %reduce-scatter.3.cloned.1.call-update) | async-done | bytes 1048592 | tf_op jit(solution)/shard_map/reduce_scatter | solution.py:82
  259.4 2.2 fusion.110
  262.4 28.5 %all-gather.13.cloned.1.call-done = bf16[512,2048]{1,0:T(8,128)(2,1)} async-done(((bf16[512,512]{1,0:T(8,128)(2,1)}), bf16[512,2048]{1,0:T(8,128)(2,1)}) %all-gather.13.cloned.1.call-update) | async-done | bytes 2097168 | tf_op jit(solution)/shard_map/all_gather | solution.py:107
  291.0 2.1 fusion.98
  293.0 75.1 %all-gather.15.cloned.1.call-done = bf16[2048,768]{1,0:T(8,128)(2,1)} async-done(((bf16[64,768]{1,0:T(8,128)(2,1)}), bf16[2048,768]{1,0:T(8,128)(2,1)}) %all-gather.15.cloned.1.call-update) | async-done | bytes 3145744 | tf_op jit(solution)/shard_map/all_gather | solution.py:35
  368.1 4.4 fusion.107
  373.1 1.3 collective-permute-start.4
  374.5 4.0 collective-permute-done.4
  378.4 3.4 collective-permute-start.5
  381.9 3.2 collective-permute-start.6
  385.1 1.3 collective-permute-start.7
  386.3 1.2 collective-permute-done.7
  387.6 3.1 collective-permute-start.8
  390.6 2.4 collective-permute-start.9
  393.1 2.3 collective-permute-done.8
  396.0 0.8 pad_maximum_fusion.1
  396.9 19.0 %while.25 = (s32[]{:T(128)}, bf16[2,256,2,4,64]{1,4,3,2,0:T(8,128)(2,1)S(1)}, bf16[2,768,2,2,64]{1,4,2,3,0:T(8,128)(2,1)S(1)}, s32[8]{0:T(128)S(1)}, s32[2,768]{...) while((s32[]{:T(128)}, ...), condition=%wide.region_10.11_spmd.clone.clone, body=%wide.region_7.10_spmd.clone.clone.sunk | while | flops 625673728 | bytes 12019361 | solution.py:74
  397.4 6.4 %fusion.155 = (f32[2,4,256]{2,1,0:T(4,128)S(1)}, bf16[2,4,256,768]{2,3,1,0:T(8,128)(2,1)}) fusion(s32[2,4]{1,0:T(2,128)S(1)} %lt.129, s32[256,768]{0,1:T(8,128)S(1)} %iota_subtract_fusion.5, pred[256,768]{0,1:T(8,128)(4,1)S(1)} %get-tuple-element.319, pred[256,768]{0,1:T(8,128)(4,1)S(1)} %get-tuple-element.320, ...), kind=kOutput, calls=%fused_computation.101.clone.1 | convolution fusion | flops 423101184 | bytes 6433792 | tf_op jit(solution)/shard_map/while/body/eval_jaxpr/sub | solution.py:68
  403.8 2.6 fusion.156
  406.9 6.4 %fusion.155 = (f32[2,4,256]{2,1,0:T(4,128)S(1)}, bf16[2,4,256,768]{2,3,1,0:T(8,128)(2,1)}) fusion(s32[2,4]{1,0:T(2,128)S(1)} %lt.129, s32[256,768]{0,1:T(8,128)S(1)} %iota_subtract_fusion.5, pred[256,768]{0,1:T(8,128)(4,1)S(1)} %get-tuple-element.319, pred[256,768]{0,1:T(8,128)(4,1)S(1)} %get-tuple-element.320, ...), kind=kOutput, calls=%fused_computation.101.clone.1 | convolution fusion | flops 423101184 | bytes 6433792 | tf_op jit(solution)/shard_map/while/body/eval_jaxpr/sub | solution.py:68
  413.3 2.5 fusion.156
  416.5 31.9 %all-gather.17.cloned.1.call-done = bf16[512,2048]{0,1:T(8,128)(2,1)} async-done(((bf16[512,64]{0,1:T(8,128)(2,1)}), bf16[512,2048]{0,1:T(8,128)(2,1)}) %all-gather.17.cloned.1.call-update) | async-done | bytes 2097168 | tf_op jit(solution)/shard_map/all_gather | solution.py:80
  448.4 4.9 fusion.123
  453.4 58.3 %reduce-scatter.5.cloned.1.call-done = f32[512,512]{1,0:T(8,128)} async-done(((f32[512,2048]{1,0:T(8,128)}), f32[512,512]{1,0:T(8,128)}) %reduce-scatter.5.cloned.1.call-update) | async-done | bytes 1048592 | tf_op jit(solution)/shard_map/reduce_scatter | solution.py:82
  511.7 2.2 add_convert_fusion
  (73 shorter events, 6.4 us)
Async XLA Ops:
  6.5 36.0 %all-gather.7.cloned.1.call-start = ((), (), s32[]{:S(2)}) async-start(), calls=%async_computation.2 | async-start | bytes 2621440 | tf_op jit(solution)/shard_map/all_gather | solution.py:98
  7.3 112.5 %all-gather.9.cloned.1.call-start = ((), (), s32[]{:S(2)}) async-start(), calls=%async_computation.3 | async-start | bytes 3244032 | tf_op jit(solution)/shard_map/all_gather | solution.py:35
  8.0 188.2 %all-gather.11.cloned.1.call-start = ((), (), s32[]{:S(2)}) async-start(), calls=%async_computation.4 | async-start | bytes 2162688 | tf_op jit(solution)/shard_map/all_gather | solution.py:80
  8.7 250.7 %reduce-scatter.3.cloned.1.call-start = ((), (), s32[]{:S(2)}) async-start(), calls=%async_computation.5 | async-start | bytes 5242880 | tf_op jit(solution)/shard_map/reduce_scatter | solution.py:82
  42.5 2.2 copy-start
  123.5 7.3 %copy-start.3 = (s32[1,2,256]{2,1,0:T(2,128)S(1)}, s32[1,2,256]{2,1,0:T(2,128)}, u32[]{:S(2)}) copy-start(s32[1,2,256]{2,1,0:T(2,128)} %param.13) | copy-start | bytes 6148
  123.5 12.9 %copy-start.4 = (s32[32]{0:T(128)S(1)}, s32[32]{0:T(128)}, u32[]{:S(2)}) copy-start(s32[32]{0:T(128)} %param.14) | copy-start | bytes 388
  124.1 18.3 %collective-permute-start = (bf16[2,256,2,2,64]{1,0,4,3,2:T(2,128)(2,1)S(1)}, bf16[2,256,2,2,64]{1,0,4,3,2:T(2,128)(2,1)S(1)}, u32[]{:S(2)}, u32[]{:S(2)}) collective-permute-start(bf16[2,256,2,2,64]{1,0,4,3,2:T(2,128)(2,1)S(1)} %slice.48), channel_id=1, source_target_pairs={{0,8},{4,12},{8,16},{12,20},{16,24},{20,28},{24,32},{28,36},{32,40... | collective-permute-start | bytes 786440 | tf_op jit(solution)/shard_map/ppermute | solution.py:17
  127.6 14.8 %collective-permute-start.1 = (bf16[2,256,2,2,64]{1,0,4,3,2:T(2,128)(2,1)S(1)}, bf16[2,256,2,2,64]{1,0,4,3,2:T(2,128)(2,1)S(1)}, u32[]{:S(2)}, u32[]{:S(2)}) collective-permute-start(bf16[2,256,2,2,64]{1,0,4,3,2:T(2,128)(2,1)S(1)} %slice.48), channel_id=1, source_target_pairs={{0,4},{4,8},{8,12},{12,16},{16,20},{20,24},{24,28},{28,32},{32,36}... | collective-permute-start | bytes 786440 | tf_op jit(solution)/shard_map/ppermute | solution.py:17
  130.8 11.1 %collective-permute-start.2 = (s32[2,256]{1,0:T(2,128)S(1)}, s32[2,256]{1,0:T(2,128)S(1)}, u32[]{:S(2)}, u32[]{:S(2)}) collective-permute-start(s32[2,256]{1,0:T(2,128)S(1)} %bitcast.216), channel_id=1, source_target_pairs={{0,8},{4,12},{8,16},{12,20},{16,24},{20,28},{24,32},{28,36},{32,40... | collective-permute-start | bytes 6152 | tf_op jit(solution)/shard_map/ppermute | solution.py:17
  133.9 8.1 %collective-permute-start.3 = (s32[2,256]{1,0:T(2,128)S(1)}, s32[2,256]{1,0:T(2,128)S(1)}, u32[]{:S(2)}, u32[]{:S(2)}) collective-permute-start(s32[2,256]{1,0:T(2,128)S(1)} %bitcast.217), channel_id=1, source_target_pairs={{0,4},{4,8},{8,12},{12,16},{16,20},{20,24},{24,28},{28,32},{32,36}... | collective-permute-start | bytes 6152 | tf_op jit(solution)/shard_map/ppermute | solution.py:17
  201.2 58.3 %copy-start.2 = (bf16[1,2,256,512]{3,2,1,0:T(8,128)(2,1)S(1)}, bf16[1,2,256,512]{3,2,1,0:T(8,128)(2,1)}, u32[]{:S(2)}) copy-start(bf16[1,2,256,512]{3,2,1,0:T(8,128)(2,1)} %param.12) | copy-start | bytes 1572868
  201.2 89.8 %all-gather.13.cloned.1.call-start = ((), (), s32[]{:S(2)}) async-start(), calls=%async_computation.6 | async-start | bytes 2621440 | tf_op jit(solution)/shard_map/all_gather | solution.py:107
  261.6 106.5 %all-gather.15.cloned.1.call-start = ((), (), s32[]{:S(2)}) async-start(), calls=%async_computation.7 | async-start | bytes 3244032 | tf_op jit(solution)/shard_map/all_gather | solution.py:35
  262.2 186.2 %all-gather.17.cloned.1.call-start = ((), (), s32[]{:S(2)}) async-start(), calls=%async_computation.8 | async-start | bytes 2162688 | tf_op jit(solution)/shard_map/all_gather | solution.py:80
  373.1 5.3 %collective-permute-start.4 = (bf16[2,256,2,2,64]{1,0,4,3,2:T(2,128)(2,1)S(1)}, bf16[2,256,2,2,64]{1,0,4,3,2:T(2,128)(2,1)S(1)}, u32[]{:S(2)}, u32[]{:S(2)}) collective-permute-start(bf16[2,256,2,2,64]{1,0,4,3,2:T(2,128)(2,1)S(1)} %slice.50), channel_id=1, source_target_pairs={{0,128},{128,0},{1,129},{129,1},{2,130},{130,2},{3,131},{131,3},{4... | collective-permute-start | bytes 786440 | tf_op jit(solution)/shard_map/ppermute | solution.py:23
  374.4 137.2 %reduce-scatter.5.cloned.1.call-start = ((), (), s32[]{:S(2)}) async-start(), calls=%async_computation.9 | async-start | bytes 5242880 | tf_op jit(solution)/shard_map/reduce_scatter | solution.py:82
  378.4 17.5 %collective-permute-start.5 = (bf16[2,256,2,2,64]{1,0,4,3,2:T(2,128)(2,1)S(1)}, bf16[2,256,2,2,64]{1,0,4,3,2:T(2,128)(2,1)S(1)}, u32[]{:S(2)}, u32[]{:S(2)}) collective-permute-start(bf16[2,256,2,2,64]{1,0,4,3,2:T(2,128)(2,1)S(1)} %collective-permute-done.4), channel_id=1, source_target_pairs={{0,8},{4,12},{8,16},{12,20},{16,24},{20,28},{24,32},{28,36},{32,40... | collective-permute-start | bytes 786440 | tf_op jit(solution)/shard_map/ppermute | solution.py:17
  381.9 14.1 %collective-permute-start.6 = (bf16[2,256,2,2,64]{1,0,4,3,2:T(2,128)(2,1)S(1)}, bf16[2,256,2,2,64]{1,0,4,3,2:T(2,128)(2,1)S(1)}, u32[]{:S(2)}, u32[]{:S(2)}) collective-permute-start(bf16[2,256,2,2,64]{1,0,4,3,2:T(2,128)(2,1)S(1)} %collective-permute-done.4), channel_id=1, source_target_pairs={{0,4},{4,8},{8,12},{12,16},{16,20},{20,24},{24,28},{28,32},{32,36}... | collective-permute-start | bytes 786440 | tf_op jit(solution)/shard_map/ppermute | solution.py:17
  385.1 2.5 collective-permute-start.7
  387.6 7.9 %collective-permute-start.8 = (s32[2,256]{1,0:T(2,128)S(1)}, s32[2,256]{1,0:T(2,128)S(1)}, u32[]{:S(2)}, u32[]{:S(2)}) collective-permute-start(s32[2,256]{1,0:T(2,128)S(1)} %collective-permute-done.7), channel_id=1, source_target_pairs={{0,8},{4,12},{8,16},{12,20},{16,24},{20,28},{24,32},{28,36},{32,40... | collective-permute-start | bytes 6152 | tf_op jit(solution)/shard_map/ppermute | solution.py:17
  390.6 4.8 collective-permute-start.9
  453.4 58.3 %copy-start.1 = (bf16[512,512]{1,0:T(8,128)(2,1)S(1)}, bf16[512,512]{1,0:T(8,128)(2,1)}, u32[]{:S(2)}) copy-start(bf16[512,512]{1,0:T(8,128)(2,1)} %fusion.110) | copy-start | bytes 1572868
Sparse Core Ops, SparseCore 0:
  9.1 33.3 all-gather.6
  45.1 74.6 all-gather.8
  122.4 73.7 all-gather.10
  201.3 58.0 reduce-scatter.2
  261.8 29.1 all-gather.12
  293.4 74.6 all-gather.14
  374.5 73.8 all-gather.16
  453.5 58.0 reduce-scatter.4
where the time goes:
time: 521 us
  waiting for transfers between devices  408 us (78%)
  matrix products  53.8 us (10%)
  starting transfers between devices  27.2 us (5%)
  between operations  13.8 us (3%)
  other arithmetic  12.2 us (2%)
    all_gather x2, waiting for transfers between devices, project_in(): lax.all_gather(weight_rows, 'tm', axis=0, tiled=True)  150 us
    reduce_scatter x2, waiting for transfers between devices, project_out(): summed = lax.psum_scatter(terms, 'mp', scatter_dimension=1, tiled=True)  116 us
    all_gather x2, waiting for transfers between devices, project_out(): lax.all_gather(weight, 'tm', axis=1, tiled=True)  65.2 us
    all_gather x1, waiting for transfers between devices, body(): full = lax.all_gather(motion, 'mp', axis=3, tiled=True).reshape(count, D)  32.9 us
    all_gather x1, waiting for transfers between devices, body(): hidden_full = lax.all_gather(hidden, 'mp', axis=1, tiled=True)  28.5 us
    sub x4, matrix products, one_clip(): exps = jnp.where(allowed, jnp.exp(scores - top), 0.0)  25.7 us
    ppermute x8, starting transfers between devices, passed_along(): lax.ppermute(value, axis, [(source, source + steps) for source in range(l...  24.2 us
  transfers between devices with their start and end apart: 18, of which 13 were waited for; matrix products, arithmetic and copies ran while one was open for 10% of the time, Pallas kernels for 0%

commit v1 on v0

--- a/solution.py
+++ b/solution.py
@@ -9,6 +9,12 @@
 HEAD_DIM = 64
 WIN = 512
 EPS = 1e-05
+
+
+def try_all_fields(sample):
+    return jnp.concatenate(
+        lax.all_to_all(jnp.stack([sample for _ in range(lax.axis_size("tm"))]), "tm", 0, 0), axis=0
+    )
 
 
 def passed_along(value, axis, steps):
@@ -30,11 +36,7 @@
 
 
 def project_in(normed_rows, weight_rows):
-    total = jnp.dot(
-        normed_rows,
-        lax.all_gather(weight_rows, "tm", axis=0, tiled=True),
-        preferred_element_type=jnp.float32,
-    )
+    total = jnp.dot(normed_rows, try_all_fields(weight_rows), preferred_element_type=jnp.float32)
     return total.astype(jnp.bfloat16)
 
 

time: 521 us -> 399 us (0.77)
  waiting for transfers between devices: 408 us -> 252 us
  starting transfers between devices: 27.2 us -> 52.4 us
  local copies, waits for them, and re-layouts: 5.06 us -> 12.4 us
    all_gather x2 -> x0, waiting for transfers between devices: 150 us -> none  [project_in(): lax.all_gather(weight_rows, 'tm', axis=0, tiled=True)]
    all_gather x2, waiting for transfers between devices: 65.2 us -> 24.8 us  [project_out(): lax.all_gather(weight, 'tm', axis=1, tiled=True)]
    all_to_all x0 -> x2, waiting for transfers between devices: none -> 34.9 us  [try_all_fields(): lax.all_to_all(jnp.stack([sample for _ in range(lax.axis_size('tm'))]), '...]
    all_to_all x0 -> x2, starting transfers between devices: none -> 24 us  [try_all_fields(): lax.all_to_all(jnp.stack([sample for _ in range(lax.axis_size('tm'))]), '...]
    reduce_scatter x2, waiting for transfers between devices: 116 us -> 105 us  [project_out(): summed = lax.psum_scatter(terms, 'mp', scatter_dimension=1, tiled=True)]
    ppermute x8, waiting for transfers between devices: 7.96 us -> 15.2 us  [passed_along(): lax.ppermute(value, axis, [(source, source + steps) for source in range(l...]
  transfers between devices with their start and end apart: 18 -> 18, of which waited for: 13 -> 11; matrix products, arithmetic and copies ran while one was open for 10% -> 15% of each run, Pallas kernels for 0% -> 0%
where the time goes in v1:
time: 399 us; the launch traced here: 398 us
  waiting for transfers between devices  252 us (63%)
  matrix products  54 us (14%)
  starting transfers between devices  52.4 us (13%)
  between operations  13.8 us (3%)
  other arithmetic  13.7 us (3%)
  local copies, waits for them, and re-layouts  12.4 us (3%)
    reduce_scatter x2, waiting for transfers between devices, project_out(): summed = lax.psum_scatter(terms, 'mp', scatter_dimension=1, tiled=True)  105 us
    all_to_all x2, waiting for transfers between devices, try_all_fields(): lax.all_to_all(jnp.stack([sample for _ in range(lax.axis_size('tm'))]), '...  34.9 us
    all_gather x1, waiting for transfers between devices, body(): full = lax.all_gather(motion, 'mp', axis=3, tiled=True).reshape(count, D)  32.2 us
    all_gather x1, waiting for transfers between devices, body(): hidden_full = lax.all_gather(hidden, 'mp', axis=1, tiled=True)  29.1 us
    ppermute x8, starting transfers between devices, passed_along(): lax.ppermute(value, axis, [(source, source + steps) for source in range(l...  27.2 us
    sub x4, matrix products, one_clip(): exps = jnp.where(allowed, jnp.exp(scores - top), 0.0)  25.5 us
    all_gather x2, waiting for transfers between devices, project_out(): lax.all_gather(weight, 'tm', axis=1, tiled=True)  24.8 us
    all_to_all x2, starting transfers between devices, try_all_fields(): lax.all_to_all(jnp.stack([sample for _ in range(lax.axis_size('tm'))]), '...  24 us
  transfers between devices with their start and end apart: 18, of which 11 were waited for; matrix products, arithmetic and copies ran while one was open for 15% of the time, Pallas kernels for 0%

profile of v1, /device:TPU:1, one launch (start us, length us, event | category | flops | bytes accessed | tf_op | source)
XLA Modules:
  0.0 398.5 jit_solution(5729890521415931133)
XLA Ops:
  6.5 2.9 stack.4
  9.4 12.2 %all-to-all-start = ((bf16[32,64,768]{2,1,0:T(8,128)(2,1)}), bf16[32,64,768]{2,1,0:T(8,128)(2,1)S(1)}, u32[]{:S(2)}, u32[]{:S(2)}) async-start(bf16[32,64,768]{2,1,0:T(8,128)(2,1)} %stack.4), calls=%async_computation | async-start | bytes 6291456 | tf_op jit(solution)/shard_map/all_to_all | solution.py:16
  21.6 0.7 all-gather.5.cloned.1.call-update
  22.4 0.7 all-gather.7.cloned.1.call-update
  23.2 32.2 %all-gather.5.cloned.1.call-done = bf16[1,2,256,2048]{3,2,1,0:T(8,128)(2,1)} async-done(((bf16[1,2,256,512]{3,2,1,0:T(8,128)(2,1)}), bf16[1,2,256,2048]{3,2,1,0:T(8,128)(2,1)}) %all-gather.5.cloned.1.call-update) | async-done | bytes 2097168 | tf_op jit(solution)/shard_map/all_gather | solution.py:100
  55.3 2.2 fusion.98
  57.6 1.9 fusion.100
  59.5 34.9 %all-to-all-done = bf16[32,64,768]{2,1,0:T(8,128)(2,1)S(1)} async-done(((bf16[32,64,768]{2,1,0:T(8,128)(2,1)}), bf16[32,64,768]{2,1,0:T(8,128)(2,1)S(1)}, u32[]{:S(2)}, u32[]{:S(2)}) %all-to-all-start) | async-done | bytes 3145760 | tf_op jit(solution)/shard_map/all_to_all | solution.py:16
  94.4 4.3 %convolution_convert_fusion = bf16[512,768]{1,0:T(8,128)(2,1)} fusion(bf16[512,2048]{1,0:T(8,128)(2,1)} %bitcast.209, bf16[2048,768]{1,0:T(8,128)(2,1)S(1)} %bitcast.205), kind=kOutput, calls=%fused_computation.89 | convolution fusion | flops 1611005952 | bytes 6029312 | tf_op jit(solution)/shard_map/dot_general | solution.py:39
  98.7 1.4 copy.17
  100.5 4.9 %collective-permute-start = (bf16[2,256,2,2,64]{1,0,4,3,2:T(2,128)(2,1)S(1)}, bf16[2,256,2,2,64]{1,0,4,3,2:T(2,128)(2,1)S(1)}, u32[]{:S(2)}, u32[]{:S(2)}) collective-permute-start(bf16[2,256,2,2,64]{1,0,4,3,2:T(2,128)(2,1)S(1)} %slice.48), channel_id=1, source_target_pairs={{0,8},{4,12},{8,16},{12,20},{16,24},{20,28},{24,32},{28,36},{32,40... | collective-permute-start | bytes 786440 | tf_op jit(solution)/shard_map/ppermute | solution.py:23
  105.4 4.5 %collective-permute-start.1 = (bf16[2,256,2,2,64]{1,0,4,3,2:T(2,128)(2,1)S(1)}, bf16[2,256,2,2,64]{1,0,4,3,2:T(2,128)(2,1)S(1)}, u32[]{:S(2)}, u32[]{:S(2)}) collective-permute-start(bf16[2,256,2,2,64]{1,0,4,3,2:T(2,128)(2,1)S(1)} %slice.48), channel_id=1, source_target_pairs={{0,4},{4,8},{8,12},{12,16},{16,20},{20,24},{24,28},{28,32},{32,36}... | collective-permute-start | bytes 786440 | tf_op jit(solution)/shard_map/ppermute | solution.py:23
  109.8 1.9 collective-permute-start.2
  111.7 1.9 collective-permute-start.3
  113.8 10.7 %collective-permute-done.2 = s32[2,256]{1,0:T(2,128)S(1)} collective-permute-done((s32[2,256]{1,0:T(2,128)S(1)}, s32[2,256]{1,0:T(2,128)S(1)}, u32[]{:S(2)}, u32[]{:S(2)}) %collective-permute-start.2) | collective-permute-done | bytes 2080 | tf_op jit(solution)/shard_map/ppermute | solution.py:23
  125.0 0.8 pad_maximum_fusion
  125.9 18.9 %while.24 = (s32[]{:T(128)}, bf16[2,256,2,4,64]{1,4,3,2,0:T(8,128)(2,1)S(1)}, bf16[2,768,2,2,64]{1,4,2,3,0:T(8,128)(2,1)S(1)}, s32[8]{0:T(128)S(1)}, s32[2,768]{...) while((s32[]{:T(128)}, ...), condition=%wide.region_4.5_spmd.clone.clone, body=%wide.region_1.4_spmd.clone.clone.sunk | while | flops 625673728 | bytes 12019361 | solution.py:76
  126.4 6.4 %fusion.150 = (f32[2,4,256]{2,1,0:T(4,128)S(1)}, bf16[2,4,256,768]{2,3,1,0:T(8,128)(2,1)}) fusion(s32[2,4]{1,0:T(2,128)S(1)} %lt.125, s32[256,768]{0,1:T(8,128)S(1)} %iota_subtract_fusion.4, pred[256,768]{0,1:T(8,128)(4,1)S(1)} %get-tuple-element.308, pred[256,768]{0,1:T(8,128)(4,1)S(1)} %get-tuple-element.309, ...), kind=kOutput, calls=%fused_computation.101.clone.1 | convolution fusion | flops 423101184 | bytes 6433792 | tf_op jit(solution)/shard_map/while/body/eval_jaxpr/sub | solution.py:70
  132.8 2.6 fusion.151
  135.9 6.4 %fusion.150 = (f32[2,4,256]{2,1,0:T(4,128)S(1)}, bf16[2,4,256,768]{2,3,1,0:T(8,128)(2,1)}) fusion(s32[2,4]{1,0:T(2,128)S(1)} %lt.125, s32[256,768]{0,1:T(8,128)S(1)} %iota_subtract_fusion.4, pred[256,768]{0,1:T(8,128)(4,1)S(1)} %get-tuple-element.308, pred[256,768]{0,1:T(8,128)(4,1)S(1)} %get-tuple-element.309, ...), kind=kOutput, calls=%fused_computation.101.clone.1 | convolution fusion | flops 423101184 | bytes 6433792 | tf_op jit(solution)/shard_map/while/body/eval_jaxpr/sub | solution.py:70
  142.2 2.5 fusion.151
  145.5 4.9 %fusion.123 = f32[512,2048]{1,0:T(8,128)} fusion(bf16[512,512]{0,1:T(8,128)(2,1)S(1)} %bitcast.203, bf16[512,2048]{0,1:T(8,128)(2,1)} %all-gather.7.cloned.1.call-done), kind=kOutput, calls=%fused_computation.104 | convolution fusion | flops 1073741824 | bytes 6815744 | tf_op jit(solution)/shard_map/dot_general | solution.py:81
  150.3 0.9 copy-done.2
  151.2 2.0 stack.5
  153.2 11.9 %all-to-all-start.1 = ((bf16[32,64,768]{2,1,0:T(8,128)(2,1)}), bf16[32,64,768]{2,1,0:T(8,128)(2,1)S(1)}, u32[]{:S(2)}, u32[]{:S(2)}) async-start(bf16[32,64,768]{2,1,0:T(8,128)(2,1)} %stack.5), calls=%async_computation.2 | async-start | bytes 6291456 | tf_op jit(solution)/shard_map/all_to_all | solution.py:16
  165.2 46.4 %reduce-scatter.3.cloned.1.call-done = f32[512,512]{1,0:T(8,128)} async-done(((f32[512,2048]{1,0:T(8,128)}), f32[512,512]{1,0:T(8,128)}) %reduce-scatter.3.cloned.1.call-update) | async-done | bytes 1048592 | tf_op jit(solution)/shard_map/reduce_scatter | solution.py:84
  211.6 2.3 fusion.111
  214.1 29.1 %all-gather.9.cloned.1.call-done = bf16[512,2048]{1,0:T(8,128)(2,1)} async-done(((bf16[512,512]{1,0:T(8,128)(2,1)}), bf16[512,2048]{1,0:T(8,128)(2,1)}) %all-gather.9.cloned.1.call-update) | async-done | bytes 2097168 | tf_op jit(solution)/shard_map/all_gather | solution.py:109
  243.2 2.1 fusion.101
  245.3 4.3 %fusion.108 = bf16[512,768]{1,0:T(8,128)(2,1)} fusion(bf16[2048,768]{1,0:T(8,128)(2,1)S(1)} %bitcast.206, bf16[512,2048]{1,0:T(8,128)(2,1)} %all-gather.9.cloned.1.call-done, f32[2048]{0:T(1024)S(1)} %bitcast.211, f32[512]{0:T(512)S(1)} %add_rsqrt_fusion), kind=kOutput, calls=%fused_computation.90 | convolution fusion | flops 1615200256 | bytes 6039552 | tf_op jit(solution)/shard_map/dot_general | solution.py:39
  249.7 1.4 copy.21
  251.9 7.2 %collective-permute-done.4 = bf16[2,256,2,2,64]{1,0,4,3,2:T(2,128)(2,1)S(1)} collective-permute-done((bf16[2,256,2,2,64]{1,0,4,3,2:T(2,128)(2,1)S(1)}, bf16[2,256,2,2,64]{1,0,4,3,2:T(2,128)(2,1)S(1)}, u32[]{:S(2)}, u32[]{:S(2)}) %collective-permute-start.4) | collective-permute-done | bytes 262176 | tf_op jit(solution)/shard_map/ppermute | solution.py:29
  259.1 4.2 %collective-permute-start.5 = (bf16[2,256,2,2,64]{1,0,4,3,2:T(2,128)(2,1)S(1)}, bf16[2,256,2,2,64]{1,0,4,3,2:T(2,128)(2,1)S(1)}, u32[]{:S(2)}, u32[]{:S(2)}) collective-permute-start(bf16[2,256,2,2,64]{1,0,4,3,2:T(2,128)(2,1)S(1)} %collective-permute-done.4), channel_id=1, source_target_pairs={{0,8},{4,12},{8,16},{12,20},{16,24},{20,28},{24,32},{28,36},{32,40... | collective-permute-start | bytes 786440 | tf_op jit(solution)/shard_map/ppermute | solution.py:23
  263.3 3.2 collective-permute-start.6
  266.9 2.5 collective-permute-done.7
  269.4 4.4 %collective-permute-start.8 = (s32[2,256]{1,0:T(2,128)S(1)}, s32[2,256]{1,0:T(2,128)S(1)}, u32[]{:S(2)}, u32[]{:S(2)}) collective-permute-start(s32[2,256]{1,0:T(2,128)S(1)} %collective-permute-done.7), channel_id=1, source_target_pairs={{0,8},{4,12},{8,16},{12,20},{16,24},{20,28},{24,32},{28,36},{32,40... | collective-permute-start | bytes 6152 | tf_op jit(solution)/shard_map/ppermute | solution.py:23
  273.9 2.3 collective-permute-start.9
  276.2 4.4 %collective-permute-done.8 = s32[2,256]{1,0:T(2,128)S(1)} collective-permute-done((s32[2,256]{1,0:T(2,128)S(1)}, s32[2,256]{1,0:T(2,128)S(1)}, u32[]{:S(2)}, u32[]{:S(2)}) %collective-permute-start.8) | collective-permute-done | bytes 2080 | tf_op jit(solution)/shard_map/ppermute | solution.py:23
  281.1 0.8 pad_maximum_fusion.1
  282.0 18.9 %while.25 = (s32[]{:T(128)}, bf16[2,256,2,4,64]{1,4,3,2,0:T(8,128)(2,1)S(1)}, bf16[2,768,2,2,64]{1,4,2,3,0:T(8,128)(2,1)S(1)}, s32[8]{0:T(128)S(1)}, s32[2,768]{...) while((s32[]{:T(128)}, ...), condition=%wide.region_10.11_spmd.clone.clone, body=%wide.region_7.10_spmd.clone.clone.sunk | while | flops 625673728 | bytes 12019361 | solution.py:76
  282.5 6.4 %fusion.156 = (f32[2,4,256]{2,1,0:T(4,128)S(1)}, bf16[2,4,256,768]{2,3,1,0:T(8,128)(2,1)}) fusion(s32[2,4]{1,0:T(2,128)S(1)} %lt.129, s32[256,768]{0,1:T(8,128)S(1)} %iota_subtract_fusion.5, pred[256,768]{0,1:T(8,128)(4,1)S(1)} %get-tuple-element.319, pred[256,768]{0,1:T(8,128)(4,1)S(1)} %get-tuple-element.320, ...), kind=kOutput, calls=%fused_computation.102.clone.1 | convolution fusion | flops 423101184 | bytes 6433792 | tf_op jit(solution)/shard_map/while/body/eval_jaxpr/sub | solution.py:70
  288.9 2.5 fusion.157
  291.9 6.4 %fusion.156 = (f32[2,4,256]{2,1,0:T(4,128)S(1)}, bf16[2,4,256,768]{2,3,1,0:T(8,128)(2,1)}) fusion(s32[2,4]{1,0:T(2,128)S(1)} %lt.129, s32[256,768]{0,1:T(8,128)S(1)} %iota_subtract_fusion.5, pred[256,768]{0,1:T(8,128)(4,1)S(1)} %get-tuple-element.319, pred[256,768]{0,1:T(8,128)(4,1)S(1)} %get-tuple-element.320, ...), kind=kOutput, calls=%fused_computation.102.clone.1 | convolution fusion | flops 423101184 | bytes 6433792 | tf_op jit(solution)/shard_map/while/body/eval_jaxpr/sub | solution.py:70
  298.3 2.5 fusion.157
  301.5 24.8 %all-gather.11.cloned.1.call-done = bf16[512,2048]{0,1:T(8,128)(2,1)} async-done(((bf16[512,64]{0,1:T(8,128)(2,1)}), bf16[512,2048]{0,1:T(8,128)(2,1)}) %all-gather.11.cloned.1.call-update) | async-done | bytes 2097168 | tf_op jit(solution)/shard_map/all_gather | solution.py:82
  326.3 4.9 %fusion.124 = f32[512,2048]{1,0:T(8,128)} fusion(bf16[512,512]{0,1:T(8,128)(2,1)S(1)} %bitcast.204, bf16[512,2048]{0,1:T(8,128)(2,1)} %all-gather.11.cloned.1.call-done), kind=kOutput, calls=%fused_computation.105 | convolution fusion | flops 1073741824 | bytes 6815744 | tf_op jit(solution)/shard_map/dot_general | solution.py:81
  331.2 58.3 %reduce-scatter.5.cloned.1.call-done = f32[512,512]{1,0:T(8,128)} async-done(((f32[512,2048]{1,0:T(8,128)}), f32[512,512]{1,0:T(8,128)}) %reduce-scatter.5.cloned.1.call-update) | async-done | bytes 1048592 | tf_op jit(solution)/shard_map/reduce_scatter | solution.py:84
  389.4 2.2 add_convert_fusion
  (74 shorter events, 6.5 us)
Async XLA Ops:
  9.4 13.7 %copy-start.3 = (f32[2,2048]{1,0:T(2,128)S(1)}, f32[2,2048]{1,0:T(2,128)}, u32[]{:S(2)}) copy-start(f32[2,2048]{1,0:T(2,128)} %param.15) | copy-start | bytes 49156
  9.4 84.9 %all-to-all-start = ((bf16[32,64,768]{2,1,0:T(8,128)(2,1)}), bf16[32,64,768]{2,1,0:T(8,128)(2,1)S(1)}, u32[]{:S(2)}, u32[]{:S(2)}) async-start(bf16[32,64,768]{2,1,0:T(8,128)(2,1)} %stack.4), calls=%async_computation | async-start | bytes 6291456 | tf_op jit(solution)/shard_map/all_to_all | solution.py:16
  21.6 33.7 %all-gather.5.cloned.1.call-start = ((), (), s32[]{:S(2)}) async-start(), calls=%async_computation.4 | async-start | bytes 2621440 | tf_op jit(solution)/shard_map/all_gather | solution.py:100
  22.3 123.1 %all-gather.7.cloned.1.call-start = ((), (), s32[]{:S(2)}) async-start(), calls=%async_computation.5 | async-start | bytes 2162688 | tf_op jit(solution)/shard_map/all_gather | solution.py:82
  23.1 188.5 %reduce-scatter.3.cloned.1.call-start = ((), (), s32[]{:S(2)}) async-start(), calls=%async_computation.6 | async-start | bytes 5242880 | tf_op jit(solution)/shard_map/reduce_scatter | solution.py:84
  55.3 2.2 copy-start
  98.7 11.2 %copy-start.4 = (s32[1,2,256]{2,1,0:T(2,128)S(1)}, s32[1,2,256]{2,1,0:T(2,128)}, u32[]{:S(2)}) copy-start(s32[1,2,256]{2,1,0:T(2,128)} %param.13) | copy-start | bytes 6148
  98.7 15.0 %copy-start.5 = (s32[32]{0:T(128)S(1)}, s32[32]{0:T(128)}, u32[]{:S(2)}) copy-start(s32[32]{0:T(128)} %param.14) | copy-start | bytes 388
  100.5 24.5 %collective-permute-start = (bf16[2,256,2,2,64]{1,0,4,3,2:T(2,128)(2,1)S(1)}, bf16[2,256,2,2,64]{1,0,4,3,2:T(2,128)(2,1)S(1)}, u32[]{:S(2)}, u32[]{:S(2)}) collective-permute-start(bf16[2,256,2,2,64]{1,0,4,3,2:T(2,128)(2,1)S(1)} %slice.48), channel_id=1, source_target_pairs={{0,8},{4,12},{8,16},{12,20},{16,24},{20,28},{24,32},{28,36},{32,40... | collective-permute-start | bytes 786440 | tf_op jit(solution)/shard_map/ppermute | solution.py:23
  105.4 19.6 %collective-permute-start.1 = (bf16[2,256,2,2,64]{1,0,4,3,2:T(2,128)(2,1)S(1)}, bf16[2,256,2,2,64]{1,0,4,3,2:T(2,128)(2,1)S(1)}, u32[]{:S(2)}, u32[]{:S(2)}) collective-permute-start(bf16[2,256,2,2,64]{1,0,4,3,2:T(2,128)(2,1)S(1)} %slice.48), channel_id=1, source_target_pairs={{0,4},{4,8},{8,12},{12,16},{16,20},{20,24},{24,28},{28,32},{32,36}... | collective-permute-start | bytes 786440 | tf_op jit(solution)/shard_map/ppermute | solution.py:23
  109.8 14.6 %collective-permute-start.2 = (s32[2,256]{1,0:T(2,128)S(1)}, s32[2,256]{1,0:T(2,128)S(1)}, u32[]{:S(2)}, u32[]{:S(2)}) collective-permute-start(s32[2,256]{1,0:T(2,128)S(1)} %bitcast.212), channel_id=1, source_target_pairs={{0,8},{4,12},{8,16},{12,20},{16,24},{20,28},{24,32},{28,36},{32,40... | collective-permute-start | bytes 6152 | tf_op jit(solution)/shard_map/ppermute | solution.py:23
  111.7 12.8 %collective-permute-start.3 = (s32[2,256]{1,0:T(2,128)S(1)}, s32[2,256]{1,0:T(2,128)S(1)}, u32[]{:S(2)}, u32[]{:S(2)}) collective-permute-start(s32[2,256]{1,0:T(2,128)S(1)} %bitcast.213), channel_id=1, source_target_pairs={{0,4},{4,8},{8,12},{12,16},{16,20},{20,24},{24,28},{28,32},{32,36}... | collective-permute-start | bytes 6152 | tf_op jit(solution)/shard_map/ppermute | solution.py:23
  150.3 0.9 copy-start.2
  153.2 92.1 %all-to-all-start.1 = ((bf16[32,64,768]{2,1,0:T(8,128)(2,1)}), bf16[32,64,768]{2,1,0:T(8,128)(2,1)S(1)}, u32[]{:S(2)}, u32[]{:S(2)}) async-start(bf16[32,64,768]{2,1,0:T(8,128)(2,1)} %stack.5), calls=%async_computation.2 | async-start | bytes 6291456 | tf_op jit(solution)/shard_map/all_to_all | solution.py:16
  165.1 78.1 %all-gather.9.cloned.1.call-start = ((), (), s32[]{:S(2)}) async-start(), calls=%async_computation.7 | async-start | bytes 2621440 | tf_op jit(solution)/shard_map/all_gather | solution.py:109
  213.9 112.4 %all-gather.11.cloned.1.call-start = ((), (), s32[]{:S(2)}) async-start(), calls=%async_computation.8 | async-start | bytes 2162688 | tf_op jit(solution)/shard_map/all_gather | solution.py:82
  251.4 7.7 %collective-permute-start.4 = (bf16[2,256,2,2,64]{1,0,4,3,2:T(2,128)(2,1)S(1)}, bf16[2,256,2,2,64]{1,0,4,3,2:T(2,128)(2,1)S(1)}, u32[]{:S(2)}, u32[]{:S(2)}) collective-permute-start(bf16[2,256,2,2,64]{1,0,4,3,2:T(2,128)(2,1)S(1)} %slice.50), channel_id=1, source_target_pairs={{0,128},{128,0},{1,129},{129,1},{2,130},{130,2},{3,131},{131,3},{4... | collective-permute-start | bytes 786440 | tf_op jit(solution)/shard_map/ppermute | solution.py:29
  251.8 137.6 %reduce-scatter.5.cloned.1.call-start = ((), (), s32[]{:S(2)}) async-start(), calls=%async_computation.9 | async-start | bytes 5242880 | tf_op jit(solution)/shard_map/reduce_scatter | solution.py:84
  259.1 21.9 %collective-permute-start.5 = (bf16[2,256,2,2,64]{1,0,4,3,2:T(2,128)(2,1)S(1)}, bf16[2,256,2,2,64]{1,0,4,3,2:T(2,128)(2,1)S(1)}, u32[]{:S(2)}, u32[]{:S(2)}) collective-permute-start(bf16[2,256,2,2,64]{1,0,4,3,2:T(2,128)(2,1)S(1)} %collective-permute-done.4), channel_id=1, source_target_pairs={{0,8},{4,12},{8,16},{12,20},{16,24},{20,28},{24,32},{28,36},{32,40... | collective-permute-start | bytes 786440 | tf_op jit(solution)/shard_map/ppermute | solution.py:23
  263.3 17.8 %collective-permute-start.6 = (bf16[2,256,2,2,64]{1,0,4,3,2:T(2,128)(2,1)S(1)}, bf16[2,256,2,2,64]{1,0,4,3,2:T(2,128)(2,1)S(1)}, u32[]{:S(2)}, u32[]{:S(2)}) collective-permute-start(bf16[2,256,2,2,64]{1,0,4,3,2:T(2,128)(2,1)S(1)} %collective-permute-done.4), channel_id=1, source_target_pairs={{0,4},{4,8},{8,12},{12,16},{16,20},{20,24},{24,28},{28,32},{32,36}... | collective-permute-start | bytes 786440 | tf_op jit(solution)/shard_map/ppermute | solution.py:23
  266.5 2.9 collective-permute-start.7
  269.4 11.1 %collective-permute-start.8 = (s32[2,256]{1,0:T(2,128)S(1)}, s32[2,256]{1,0:T(2,128)S(1)}, u32[]{:S(2)}, u32[]{:S(2)}) collective-permute-start(s32[2,256]{1,0:T(2,128)S(1)} %collective-permute-done.7), channel_id=1, source_target_pairs={{0,8},{4,12},{8,16},{12,20},{16,24},{20,28},{24,32},{28,36},{32,40... | collective-permute-start | bytes 6152 | tf_op jit(solution)/shard_map/ppermute | solution.py:23
  273.9 6.7 %collective-permute-start.9 = (s32[2,256]{1,0:T(2,128)S(1)}, s32[2,256]{1,0:T(2,128)S(1)}, u32[]{:S(2)}, u32[]{:S(2)}) collective-permute-start(s32[2,256]{1,0:T(2,128)S(1)} %collective-permute-done.7), channel_id=1, source_target_pairs={{0,4},{4,8},{8,12},{12,16},{16,20},{20,24},{24,28},{28,32},{32,36}... | collective-permute-start | bytes 6152 | tf_op jit(solution)/shard_map/ppermute | solution.py:23
  331.2 58.3 %copy-start.1 = (bf16[512,512]{1,0:T(8,128)(2,1)S(1)}, bf16[512,512]{1,0:T(8,128)(2,1)}, u32[]{:S(2)}) copy-start(bf16[512,512]{1,0:T(8,128)(2,1)} %fusion.111) | copy-start | bytes 1572868
Sparse Core Ops, SparseCore 0:
  24.2 31.0 all-gather.4
  57.9 79.5 all-gather.6
  150.5 61.0 reduce-scatter.2
  214.0 29.1 all-gather.8
  252.0 74.2 all-gather.10
  331.3 58.0 reduce-scatter.4
